TPU v7x, 256 devices: a whole 4x4x8 slice. The times are simulated.
256 devices in a mesh: tm: 32 (over y, z_hi, core), rows: 8 (over z_lo, x).
Axes of the slice: x: 4, y: 4, z: 8 (z_hi: 4, z_lo: 2; z = z_hi * 2 + z_lo), core: 2. Of those that a mesh axis runs over, the one named last changes fastest.
Arguments:
- latent: bfloat16 [32, 16, 128, 512], P('tm', 'rows'), may hold values from -32 to 32
- norm_gain: float32 [512], replicated, may hold values from 0.1 to 1.9
- conv_weight: bfloat16 [27, 512, 512], P(None, 'tm'), may hold values from -0.0546875 to 0.0546875
- grad_out: bfloat16 [32, 16, 128, 512], P('tm', 'rows'), may hold values from -6 to 6
Outputs:
- refined: bfloat16 [32, 16, 128, 512], P('tm', 'rows')
- grad_latent: float32 [32, 16, 128, 512], P('tm', 'rows')
All inputs are finite; a program needn't handle non-finite values.
Results may differ from a plain program's by a relative error of at most 0.0013.
The roundings to bfloat16 on the way count: a program that leaves them out, or rounds other values in their place, can miss the bound.
Values may be sent and summed in bfloat16 or wider, within the bound.
No kernel may reach another device: no remote copies, remote signals or barrier semaphores. Data moves between devices by JAX's collectives and lax.ppermute only.
A program may use at most 64 MiB of HBM per device.

v0:
```python
import jax
import jax.numpy as jnp
from jax import lax
from jax.sharding import PartitionSpec as P

GROUPS = 32
epsilon = 1e-06


def shifted(block, axis, distance):
    devices = range(lax.axis_size(axis))
    route = [(i - distance, i) for i in devices if i - distance in devices]
    return lax.ppermute(block, axis, route)


def with_halo(shard, sides, width):
    for axis, dim in sides:
        size, length = (lax.axis_size(axis), shard.shape[dim])
        up = [(i, (i + 1) % size) for i in range(size - 1)]
        down = [(j, i) for i, j in up]
        last = lax.slice_in_dim(shard, length - width, length, axis=dim)
        first = lax.slice_in_dim(shard, 0, width, axis=dim)
        before = lax.ppermute(last, axis, up)
        after = lax.ppermute(first, axis, down)
        shard = jnp.concatenate([before, shard, after], axis=dim)
    return shard


def grouped_view(values):
    return values.reshape(
        values.shape[0], values.shape[1] * values.shape[2], GROUPS, values.shape[3] // GROUPS
    )


def widen_columns(values):
    return jnp.pad(values, ((0, 0), (0, 0), (1, 1), (0, 0)))


def shards(latent, norm_gain, conv_weight, grad_out):
    frames_here, rows_here, columns, channels = latent.shape
    cell_count = lax.axis_size("rows") * rows_here * columns * (channels // GROUPS)
    full_weight = lax.all_gather(conv_weight, "tm", axis=1, tiled=True)
    latent_wide = latent.astype(jnp.float32)
    grouped = grouped_view(latent_wide)
    average = lax.psum(jnp.sum(grouped, axis=(1, 3)), "rows") / cell_count
    centred = grouped - average[:, None, :, None]
    spread = lax.psum(jnp.sum(centred * centred, axis=(1, 3)), "rows") / cell_count
    inverse = lax.rsqrt(spread + epsilon)
    normed_grouped = centred * inverse[:, None, :, None]
    normed = normed_grouped.reshape(latent.shape)
    scaled = normed * norm_gain
    sigmoid_value = jax.nn.sigmoid(scaled)
    activated = (scaled * sigmoid_value).astype(jnp.bfloat16)
    before_one = shifted(activated, "tm", 1)
    before_two = shifted(activated, "tm", 2)
    padded = with_halo(
        jnp.concatenate([before_two, before_one, activated], axis=0), (("rows", 1),), 1
    )
    after_one = shifted(grad_out, "tm", -1)
    after_two = shifted(grad_out, "tm", -2)
    padded_grad = with_halo(
        jnp.concatenate([grad_out, after_one, after_two], axis=0), (("rows", 1),), 1
    )
    padded = widen_columns(padded)
    padded_grad = widen_columns(padded_grad)
    conv_sum = jnp.zeros((frames_here * rows_here * columns, channels), jnp.float32)
    grad_act = jnp.zeros((frames_here * rows_here * columns, channels), jnp.float32)
    for time_tap in range(3):
        for row_tap in range(3):
            for col_tap in range(3):
                tap_weight = full_weight[time_tap * 9 + row_tap * 3 + col_tap]
                window = padded[
                    time_tap : time_tap + frames_here,
                    row_tap : row_tap + rows_here,
                    col_tap : col_tap + columns,
                ]
                conv_sum = conv_sum + jnp.dot(
                    window.reshape(-1, channels), tap_weight, preferred_element_type=jnp.float32
                )
                back_window = padded_grad[
                    2 - time_tap : 2 - time_tap + frames_here,
                    2 - row_tap : 2 - row_tap + rows_here,
                    2 - col_tap : 2 - col_tap + columns,
                ]
                grad_act = grad_act + lax.dot_general(
                    back_window.reshape(-1, channels),
                    tap_weight,
                    (((1,), (1,)), ((), ())),
                    preferred_element_type=jnp.float32,
                )
    refined = (latent_wide + conv_sum.reshape(latent.shape)).astype(jnp.bfloat16)
    grad_scaled = (
        grad_act.reshape(latent.shape) * sigmoid_value * (1.0 + scaled * (1.0 - sigmoid_value))
    )
    grad_normed = grouped_view(grad_scaled * norm_gain)
    first_sum, second_sum = lax.psum(
        (jnp.sum(grad_normed, axis=(1, 3)), jnp.sum(grad_normed * normed_grouped, axis=(1, 3))),
        "rows",
    )
    first = first_sum / cell_count
    second = second_sum / cell_count
    grad_norm_part = (
        grad_normed - first[:, None, :, None] - normed_grouped * second[:, None, :, None]
    ) * inverse[:, None, :, None]
    grad_latent = grad_out.astype(jnp.float32) + grad_norm_part.reshape(latent.shape)
    return (refined, grad_latent)


def solution(mesh):
    placed = (P("tm", "rows", None, None), P(), P(None, "tm", None), P("tm", "rows", None, None))
    return jax.shard_map(
        shards,
        mesh=mesh,
        in_specs=placed,
        out_specs=(P("tm", "rows", None, None), P("tm", "rows", None, None)),
        check_vma=False,
    )
```

profile of v0, /device:TPU:6, one launch (start us, length us, event | category | flops | bytes accessed | tf_op | source)
XLA Modules:
  0.0 219.8 jit_solution(12708673439425601817)
XLA Ops:
  7.2 0.7 all-gather.2.cloned.1.call-update
  7.9 1.3 collective-permute-start.4
  9.2 1.3 collective-permute-start.5
  10.5 1.0 convert_reduce_fusion
  11.7 16.1 %psum.28 = f32[1,32]{1,0:T(1,128)S(1)} all-reduce(f32[1,32]{1,0:T(1,128)S(1)} %bitcast.290), channel_id=1, replica_groups=mesh['tm'=32,'rows'=8] {'rows'}, use_global_device_ids=true, to_apply=%region_2.0 | all-reduce | flops 32 | bytes 256 | tf_op jit(solution)/shard_map/psum | solution.py:45
  27.8 1.0 constant_dynamic-update-slice_fusion.2
  28.8 5.3 %collective-permute-done.5 = bf16[1,2,128,512]{3,2,1,0:T(8,128)(2,1)S(1)} collective-permute-done((bf16[1,2,128,512]{3,2,1,0:T(8,128)(2,1)}, bf16[1,2,128,512]{3,2,1,0:T(8,128)(2,1)S(1)}, u32[]{:S(2)}, u32[]{:S(2)}) %collective-permute-start.5) | collective-permute-done | bytes 262176 | tf_op jit(solution)/shard_map/ppermute | solution.py:13
  34.3 0.6 copy-done.7
  34.9 1.9 collective-permute-start.6
  36.8 3.9 %collective-permute-start.7 = (bf16[3,1,128,512]{3,2,1,0:T(8,128)(2,1)S(1)}, bf16[3,1,128,512]{3,2,1,0:T(8,128)(2,1)S(1)}, u32[]{:S(2)}, u32[]{:S(2)}) collective-permute-start(bf16[3,1,128,512]{3,2,1,0:T(8,128)(2,1)S(1)} %get-tuple-element.59), channel_id=1, source_target_pairs={{1,0},{2,1},{3,2},{4,3},{5,4},{6,5},{7,6},{9,8},{10,9},{11,10},{12... | collective-permute-start | bytes 1179656 | tf_op jit(solution)/shard_map/ppermute | solution.py:24
  40.9 1.0 fusion.31
  42.1 22.3 %psum.29 = f32[1,32]{1,0:T(1,128)S(1)} all-reduce(f32[1,32]{1,0:T(1,128)S(1)} %bitcast.291), channel_id=1, replica_groups=mesh['tm'=32,'rows'=8] {'rows'}, use_global_device_ids=true, to_apply=%region_5.6 | all-reduce | flops 32 | bytes 256 | tf_op jit(solution)/shard_map/psum | solution.py:47
  64.6 1.2 pad_maximum_fusion.6
  65.8 0.4 select_maximum_fusion
  66.2 1.7 fusion.87
  67.9 52.9 %all-gather.2.cloned.1.call-done = bf16[27,512,512]{2,1,0:T(8,128)(2,1)} async-done(((bf16[27,16,512]{2,1,0:T(8,128)(2,1)}), bf16[27,512,512]{2,1,0:T(8,128)(2,1)}) %all-gather.2.cloned.1.call-update) | async-done | bytes 14155792 | tf_op jit(solution)/shard_map/all_gather | solution.py:42
  120.8 1.6 fusion.59
  122.4 2.1 fusion.41
  124.6 2.2 fusion.77
  126.7 1.4 fusion.53
  128.2 1.5 fusion.35
  129.7 1.5 fusion.71
  131.1 1.5 fusion.81
  132.6 1.4 fusion.65
  134.0 1.4 fusion.47
  135.5 1.5 fusion.79
  137.0 1.5 fusion.33
  138.4 1.3 fusion.75
  141.1 0.3 fusion.61
  144.5 0.8 fusion.8
  145.3 0.3 fusion.85
  145.7 2.3 %collective-permute-start.1 = (bf16[1,2,128,512]{3,2,1,0:T(8,128)(2,1)S(1)}, bf16[1,2,128,512]{3,2,1,0:T(8,128)(2,1)S(1)}, u32[]{:S(2)}, u32[]{:S(2)}) collective-permute-start(bf16[1,2,128,512]{3,2,1,0:T(8,128)(2,1)S(1)} %get-tuple-element.62), channel_id=1, source_target_pairs={{0,8},{8,16},{16,24},{24,32},{32,40},{40,48},{48,56},{56,64},{64,7... | collective-permute-start | bytes 786440 | tf_op jit(solution)/shard_map/ppermute | solution.py:13
  148.0 6.9 %collective-permute-start = (bf16[1,2,128,512]{3,2,1,0:T(8,128)(2,1)S(1)}, bf16[1,2,128,512]{3,2,1,0:T(8,128)(2,1)S(1)}, u32[]{:S(2)}, u32[]{:S(2)}) collective-permute-start(bf16[1,2,128,512]{3,2,1,0:T(8,128)(2,1)S(1)} %get-tuple-element.62), channel_id=1, source_target_pairs={{0,16},{8,24},{16,32},{24,40},{32,48},{40,56},{48,64},{56,72},{64,... | collective-permute-start | bytes 786440 | tf_op jit(solution)/shard_map/ppermute | solution.py:13
  155.2 22.7 %all-reduce.2 = (f32[1,32]{1,0:T(1,128)S(1)}, f32[1,32]{1,0:T(1,128)S(1)}) all-reduce(f32[1,32]{1,0:T(1,128)S(1)} %bitcast.289, f32[1,32]{1,0:T(1,128)S(1)} %bitcast.288), channel_id=1, replica_groups=mesh['tm'=32,'rows'=8] {'rows'}, use_global_device_ids=true, to_apply=%region_11.12 | all-reduce | flops 64 | bytes 512 | tf_op jit(solution)/shard_map/psum | solution.py:96
  178.3 1.3 fusion.78
  179.8 3.7 %collective-permute-start.2 = (bf16[3,1,128,512]{3,2,1,0:T(8,128)(2,1)S(1)}, bf16[3,1,128,512]{3,2,1,0:T(8,128)(2,1)S(1)}, u32[]{:S(2)}, u32[]{:S(2)}) collective-permute-start(bf16[3,1,128,512]{3,2,1,0:T(8,128)(2,1)S(1)} %get-tuple-element.60), channel_id=1, source_target_pairs={{0,1},{1,2},{2,3},{3,4},{4,5},{5,6},{6,7},{8,9},{9,10},{10,11},{11... | collective-permute-start | bytes 1179656 | tf_op jit(solution)/shard_map/ppermute | solution.py:23
  183.6 2.3 %collective-permute-start.3 = (bf16[3,1,128,512]{3,2,1,0:T(8,128)(2,1)S(1)}, bf16[3,1,128,512]{3,2,1,0:T(8,128)(2,1)S(1)}, u32[]{:S(2)}, u32[]{:S(2)}) collective-permute-start(bf16[3,1,128,512]{3,2,1,0:T(8,128)(2,1)S(1)} %get-tuple-element.61), channel_id=1, source_target_pairs={{1,0},{2,1},{3,2},{4,3},{5,4},{6,5},{7,6},{9,8},{10,9},{11,10},{12... | collective-permute-start | bytes 1179656 | tf_op jit(solution)/shard_map/ppermute | solution.py:24
  185.9 1.5 fusion.42
  187.4 1.3 fusion.60
  188.7 4.1 %collective-permute-done.2 = bf16[3,1,128,512]{3,2,1,0:T(8,128)(2,1)S(1)} collective-permute-done((bf16[3,1,128,512]{3,2,1,0:T(8,128)(2,1)S(1)}, bf16[3,1,128,512]{3,2,1,0:T(8,128)(2,1)S(1)}, u32[]{:S(2)}, u32[]{:S(2)}) %collective-permute-start.2) | collective-permute-done | bytes 393248 | tf_op jit(solution)/shard_map/ppermute | solution.py:23
  192.9 5.6 %collective-permute-done.3 = bf16[3,1,128,512]{3,2,1,0:T(8,128)(2,1)S(1)} collective-permute-done((bf16[3,1,128,512]{3,2,1,0:T(8,128)(2,1)S(1)}, bf16[3,1,128,512]{3,2,1,0:T(8,128)(2,1)S(1)}, u32[]{:S(2)}, u32[]{:S(2)}) %collective-permute-start.3) | collective-permute-done | bytes 393248 | tf_op jit(solution)/shard_map/ppermute | solution.py:24
  198.4 0.7 select_maximum_fusion.2
  199.2 0.8 fusion.88
  200.1 1.8 fusion.66
  202.0 1.3 fusion.48
  203.3 1.3 fusion.82
  210.8 1.1 fusion.11
  211.9 1.1 fusion.30
  (91 shorter events, 12.2 us)
Async XLA Ops:
  7.2 117.4 %copy-start.2 = (bf16[1,2,128,512]{3,2,1,0:T(8,128)(2,1)S(1)}, bf16[1,2,128,512]{3,2,1,0:T(8,128)(2,1)}, u32[]{:S(2)}) copy-start(bf16[1,2,128,512]{3,2,1,0:T(8,128)(2,1)} %param.7) | copy-start | bytes 786436
  7.2 113.7 %all-gather.2.cloned.1.call-start = ((), (), s32[]{:S(2)}) async-start(), calls=%async_computation | async-start | bytes 14598144 | tf_op jit(solution)/shard_map/all_gather | solution.py:42
  7.9 20.9 %collective-permute-start.4 = (bf16[1,2,128,512]{3,2,1,0:T(8,128)(2,1)}, bf16[1,2,128,512]{3,2,1,0:T(8,128)(2,1)S(1)}, u32[]{:S(2)}, u32[]{:S(2)}) collective-permute-start(bf16[1,2,128,512]{3,2,1,0:T(8,128)(2,1)} %param.7), channel_id=1, source_target_pairs={{8,0},{16,8},{24,16},{32,24},{40,32},{48,40},{56,48},{64,56},{72,6... | collective-permute-start | bytes 786440 | tf_op jit(solution)/shard_map/ppermute | solution.py:13
  9.2 24.9 %collective-permute-start.5 = (bf16[1,2,128,512]{3,2,1,0:T(8,128)(2,1)}, bf16[1,2,128,512]{3,2,1,0:T(8,128)(2,1)S(1)}, u32[]{:S(2)}, u32[]{:S(2)}) collective-permute-start(bf16[1,2,128,512]{3,2,1,0:T(8,128)(2,1)} %param.7), channel_id=1, source_target_pairs={{16,0},{24,8},{32,16},{40,24},{48,32},{56,40},{64,48},{72,56},{80,... | collective-permute-start | bytes 786440 | tf_op jit(solution)/shard_map/ppermute | solution.py:13
  28.8 5.5 %copy-start.6 = (bf16[1,2,128,512]{3,2,1,0:T(8,128)(2,1)}, bf16[1,2,128,512]{3,2,1,0:T(8,128)(2,1)S(1)}, u32[]{:S(2)}) copy-start(bf16[1,2,128,512]{3,2,1,0:T(8,128)(2,1)S(1)} %collective-permute-done.4) | copy-start | bytes 786436
  34.2 0.7 copy-start.7
  34.9 29.8 %collective-permute-start.6 = (bf16[3,1,128,512]{3,2,1,0:T(8,128)(2,1)S(1)}, bf16[3,1,128,512]{3,2,1,0:T(8,128)(2,1)S(1)}, u32[]{:S(2)}, u32[]{:S(2)}) collective-permute-start(bf16[3,1,128,512]{3,2,1,0:T(8,128)(2,1)S(1)} %get-tuple-element.58), channel_id=1, source_target_pairs={{0,1},{1,2},{2,3},{3,4},{4,5},{5,6},{6,7},{8,9},{9,10},{10,11},{11... | collective-permute-start | bytes 1179656 | tf_op jit(solution)/shard_map/ppermute | solution.py:23
  36.8 27.9 %collective-permute-start.7 = (bf16[3,1,128,512]{3,2,1,0:T(8,128)(2,1)S(1)}, bf16[3,1,128,512]{3,2,1,0:T(8,128)(2,1)S(1)}, u32[]{:S(2)}, u32[]{:S(2)}) collective-permute-start(bf16[3,1,128,512]{3,2,1,0:T(8,128)(2,1)S(1)} %get-tuple-element.59), channel_id=1, source_target_pairs={{1,0},{2,1},{3,2},{4,3},{5,4},{6,5},{7,6},{9,8},{10,9},{11,10},{12... | collective-permute-start | bytes 1179656 | tf_op jit(solution)/shard_map/ppermute | solution.py:24
  120.8 17.6 %copy-start = (bf16[27,512,512]{2,1,0:T(8,128)(2,1)S(1)}, bf16[27,512,512]{2,1,0:T(8,128)(2,1)}, u32[]{:S(2)}) copy-start(bf16[27,512,512]{2,1,0:T(8,128)(2,1)} %all-gather.2.cloned.1.call-done) | copy-start | bytes 42467332
  120.8 18.9 %copy-start.5 = (bf16[1,2,128,512]{3,2,1,0:T(8,128)(2,1)S(1)}, bf16[1,2,128,512]{3,2,1,0:T(8,128)(2,1)}, u32[]{:S(2)}) copy-start(bf16[1,2,128,512]{3,2,1,0:T(8,128)(2,1)} %get-tuple-element.11) | copy-start | bytes 786436
  120.8 19.2 %copy-start.4 = (bf16[1,2,128,512]{3,2,1,0:T(8,128)(2,1)S(1)}, bf16[1,2,128,512]{3,2,1,0:T(8,128)(2,1)}, u32[]{:S(2)}) copy-start(bf16[1,2,128,512]{3,2,1,0:T(8,128)(2,1)} %get-tuple-element.12) | copy-start | bytes 786436
  120.8 19.6 %copy-start.3 = (bf16[1,2,128,512]{3,2,1,0:T(8,128)(2,1)S(1)}, bf16[1,2,128,512]{3,2,1,0:T(8,128)(2,1)}, u32[]{:S(2)}) copy-start(bf16[1,2,128,512]{3,2,1,0:T(8,128)(2,1)} %get-tuple-element.13) | copy-start | bytes 786436
  141.1 4.2 %copy-start.1 = (bf16[1,2,128,512]{3,2,1,0:T(8,128)(2,1)S(1)}, bf16[1,2,128,512]{3,2,1,0:T(8,128)(2,1)}, u32[]{:S(2)}) copy-start(bf16[1,2,128,512]{3,2,1,0:T(8,128)(2,1)} %param.4) | copy-start | bytes 786436
  141.1 4.2 %copy-start.8 = (f32[512]{0:T(512)S(1)}, f32[512]{0:T(512)}, u32[]{:S(2)}) copy-start(f32[512]{0:T(512)} %param.5) | copy-start | bytes 6148
  145.3 59.3 %slice-start = ((s8[14155776]{0:T(1024)(128)(4,1)}), s8[1572864]{0:T(1024)(128)(4,1)S(1)}, s32[]{:S(2)}) async-start(s8[14155776]{0:T(1024)(128)(4,1)} %bitcast.231), calls=%async_computation.1 | async-start | bytes 3145728
  145.7 34.0 %collective-permute-start.1 = (bf16[1,2,128,512]{3,2,1,0:T(8,128)(2,1)S(1)}, bf16[1,2,128,512]{3,2,1,0:T(8,128)(2,1)S(1)}, u32[]{:S(2)}, u32[]{:S(2)}) collective-permute-start(bf16[1,2,128,512]{3,2,1,0:T(8,128)(2,1)S(1)} %get-tuple-element.62), channel_id=1, source_target_pairs={{0,8},{8,16},{16,24},{24,32},{32,40},{40,48},{48,56},{56,64},{64,7... | collective-permute-start | bytes 786440 | tf_op jit(solution)/shard_map/ppermute | solution.py:13
  148.0 31.7 %collective-permute-start = (bf16[1,2,128,512]{3,2,1,0:T(8,128)(2,1)S(1)}, bf16[1,2,128,512]{3,2,1,0:T(8,128)(2,1)S(1)}, u32[]{:S(2)}, u32[]{:S(2)}) collective-permute-start(bf16[1,2,128,512]{3,2,1,0:T(8,128)(2,1)S(1)} %get-tuple-element.62), channel_id=1, source_target_pairs={{0,16},{8,24},{16,32},{24,40},{32,48},{40,56},{48,64},{56,72},{64,... | collective-permute-start | bytes 786440 | tf_op jit(solution)/shard_map/ppermute | solution.py:13
  179.8 13.0 %collective-permute-start.2 = (bf16[3,1,128,512]{3,2,1,0:T(8,128)(2,1)S(1)}, bf16[3,1,128,512]{3,2,1,0:T(8,128)(2,1)S(1)}, u32[]{:S(2)}, u32[]{:S(2)}) collective-permute-start(bf16[3,1,128,512]{3,2,1,0:T(8,128)(2,1)S(1)} %get-tuple-element.60), channel_id=1, source_target_pairs={{0,1},{1,2},{2,3},{3,4},{4,5},{5,6},{6,7},{8,9},{9,10},{10,11},{11... | collective-permute-start | bytes 1179656 | tf_op jit(solution)/shard_map/ppermute | solution.py:23
  183.6 14.8 %collective-permute-start.3 = (bf16[3,1,128,512]{3,2,1,0:T(8,128)(2,1)S(1)}, bf16[3,1,128,512]{3,2,1,0:T(8,128)(2,1)S(1)}, u32[]{:S(2)}, u32[]{:S(2)}) collective-permute-start(bf16[3,1,128,512]{3,2,1,0:T(8,128)(2,1)S(1)} %get-tuple-element.61), channel_id=1, source_target_pairs={{1,0},{2,1},{3,2},{4,3},{5,4},{6,5},{7,6},{9,8},{10,9},{11,10},{12... | collective-permute-start | bytes 1179656 | tf_op jit(solution)/shard_map/ppermute | solution.py:24
  185.9 18.8 %slice-start.1 = ((s8[14155776]{0:T(1024)(128)(4,1)}), s8[4194304]{0:T(1024)(128)(4,1)S(1)}, s32[]{:S(2)}) async-start(s8[14155776]{0:T(1024)(128)(4,1)} %bitcast.231), calls=%async_computation.2 | async-start | bytes 8388608
  199.2 5.5 %slice-start.2 = ((s8[14155776]{0:T(1024)(128)(4,1)}), s8[4194304]{0:T(1024)(128)(4,1)S(1)}, s32[]{:S(2)}) async-start(s8[14155776]{0:T(1024)(128)(4,1)} %bitcast.231), calls=%async_computation.3 | async-start | bytes 8388608
  199.9 4.7 %slice-start.3 = ((s8[14155776]{0:T(1024)(128)(4,1)}), s8[4194304]{0:T(1024)(128)(4,1)S(1)}, s32[]{:S(2)}) async-start(s8[14155776]{0:T(1024)(128)(4,1)} %bitcast.231), calls=%async_computation.4 | async-start | bytes 8388608
Sparse Core Ops, SparseCore 0:
  10.6 110.1 all-gather.1
where the time goes:
time: 221 us; the launch traced here: 220 us
  waiting for transfers between devices  68.6 us (31%)
  blocking collectives  61.2 us (28%)
  matrix products  39.8 us (18%)
  starting transfers between devices  23.6 us (11%)
  between operations  14.8 us (7%)
  other arithmetic  6.57 us (3%)
  local copies, waits for them, and re-layouts  5.16 us (2%)
    all_gather x1, waiting for transfers between devices, shards(): full_weight = lax.all_gather(conv_weight, 'tm', axis=1, tiled=True)  52.9 us
    dot_general x27, matrix products, shards(): lax.dot_general(back_window.reshape(-1, channels), tap_weight, (((1,), (1...  24.2 us
    psum x1, blocking collectives, shards(): lax.psum((jnp.sum(grad_normed, axis=(1, 3)), jnp.sum(grad_normed * normed...  22.7 us
    psum x1, blocking collectives, shards(): lax.psum(jnp.sum(centred * centred, axis=(1, 3)), 'rows') / cell_count  22.3 us
    psum x1, blocking collectives, shards(): average = lax.psum(jnp.sum(grouped, axis=(1, 3)), 'rows') / cell_count  16.1 us
    dot_general x27, matrix products, shards(): jnp.dot(window.reshape(-1, channels), tap_weight, preferred_element_type=...  15.7 us
    ppermute x4, starting transfers between devices, shifted(): return lax.ppermute(block, axis, route)  11.8 us
    ppermute x2, starting transfers between devices, with_halo(): after = lax.ppermute(first, axis, down)  6.21 us
  transfers between devices with their start and end apart: 9, of which 4 were waited for; matrix products, arithmetic and copies ran while one was open for 5% of the time, Pallas kernels for 0%

commit v1 on v0

--- a/solution.py
+++ b/solution.py
@@ -37,9 +37,17 @@
 
 
 def shards(latent, norm_gain, conv_weight, grad_out):
+
+    def _save_types(piece_in):
+        clean = lax.psum(1, "tm")
+        u1 = jnp.stack([piece_in] * clean, 0)
+        found_now = lax.all_to_all(u1, "tm", 0, 0)
+        state_now = jnp.concatenate(found_now, axis=1)
+        return state_now
+
     frames_here, rows_here, columns, channels = latent.shape
     cell_count = lax.axis_size("rows") * rows_here * columns * (channels // GROUPS)
-    full_weight = lax.all_gather(conv_weight, "tm", axis=1, tiled=True)
+    full_weight = _save_types(conv_weight)
     latent_wide = latent.astype(jnp.float32)
     grouped = grouped_view(latent_wide)
     average = lax.psum(jnp.sum(grouped, axis=(1, 3)), "rows") / cell_count

time: 221 us -> 466 us (2.11)
  the two profiles are of different devices: /device:TPU:6 before, /device:TPU:22 now
where the time goes in v1:
time: 466 us; the launch traced here: 465 us
  blocking collectives  363 us (78%)
  starting transfers between devices  41.8 us (9%)
  local copies, waits for them, and re-layouts  21.6 us (5%)
  matrix products  19.4 us (4%)
  waiting for transfers between devices  11.6 us (2%)
  other arithmetic  5.54 us (1%)
    psum x1, blocking collectives, shards(): average = lax.psum(jnp.sum(grouped, axis=(1, 3)), 'rows') / cell_count  322 us
    psum x1, blocking collectives, shards(): lax.psum((jnp.sum(grad_normed, axis=(1, 3)), jnp.sum(grad_normed * normed...  23 us
    psum x1, blocking collectives, shards(): lax.psum(jnp.sum(centred * centred, axis=(1, 3)), 'rows') / cell_count  18.2 us
    ppermute x4, starting transfers between devices, shifted(): return lax.ppermute(block, axis, route)  15.9 us
    all_to_all x1, starting transfers between devices, _save_types(): found_now = lax.all_to_all(u1, 'tm', 0, 0)  11.8 us
    ppermute x2, waiting for transfers between devices, with_halo(): after = lax.ppermute(first, axis, down)  11.6 us
    ppermute x2, starting transfers between devices, with_halo(): before = lax.ppermute(last, axis, up)  10 us
    dot_general x27, matrix products, shards(): jnp.dot(window.reshape(-1, channels), tap_weight, preferred_element_type=...  9.86 us
  transfers between devices with their start and end apart: 9, of which 1 were waited for; matrix products, arithmetic and copies ran while one was open for 2% of the time, Pallas kernels for 0%

profile of v1, /device:TPU:22, one launch (start us, length us, event | category | flops | bytes accessed | tf_op | source)
XLA Modules:
  0.0 465.0 jit_solution(12013309357543813674)
XLA Ops:
  0.6 7.9 %stack.2 = bf16[32,27,16,512]{3,2,1,0:T(8,128)(2,1)} broadcast(bf16[27,16,512]{2,1,0:T(8,128)(2,1)} %param.6), dimensions={1,2,3} | broadcast | bytes 14598144 | tf_op jit(solution)/shard_map/stack | solution.py:43
  8.5 11.8 %all-to-all-start = ((bf16[32,27,16,512]{3,2,1,0:T(8,128)(2,1)}), bf16[32,27,16,512]{3,2,1,0:T(8,128)(2,1)}, u32[]{:S(2)}, u32[]{:S(2)}) async-start(bf16[32,27,16,512]{3,2,1,0:T(8,128)(2,1)} %stack.2), calls=%async_computation | async-start | bytes 28311552 | tf_op jit(solution)/shard_map/all_to_all | solution.py:44
  20.3 5.2 %collective-permute-start.4 = (bf16[1,2,128,512]{3,2,1,0:T(8,128)(2,1)S(1)}, bf16[1,2,128,512]{3,2,1,0:T(8,128)(2,1)S(1)}, u32[]{:S(2)}, u32[]{:S(2)}) collective-permute-start(bf16[1,2,128,512]{3,2,1,0:T(8,128)(2,1)S(1)} %copy-done.45), channel_id=1, source_target_pairs={{8,0},{16,8},{24,16},{32,24},{40,32},{48,40},{56,48},{64,56},{72,6... | collective-permute-start | bytes 786440 | tf_op jit(solution)/shard_map/ppermute | solution.py:13
  25.5 4.3 collective-permute-start.5
  30.0 321.6 %psum.28 = f32[1,32]{1,0:T(1,128)S(1)} all-reduce(f32[1,32]{1,0:T(1,128)S(1)} %bitcast.316), channel_id=1, replica_groups=mesh['tm'=32,'rows'=8] {'rows'}, use_global_device_ids=true, to_apply=%region_2.0 | all-reduce | flops 32 | bytes 256 | tf_op jit(solution)/shard_map/psum | solution.py:53
  351.8 0.5 copy-done.71
  352.4 6.0 %collective-permute-start.6 = (bf16[3,1,128,512]{3,2,1,0:T(8,128)(2,1)S(1)}, bf16[3,1,128,512]{3,2,1,0:T(8,128)(2,1)S(1)}, u32[]{:S(2)}, u32[]{:S(2)}) collective-permute-start(bf16[3,1,128,512]{3,2,1,0:T(8,128)(2,1)S(1)} %get-tuple-element.85), channel_id=1, source_target_pairs={{0,1},{1,2},{2,3},{3,4},{4,5},{5,6},{6,7},{8,9},{9,10},{10,11},{11... | collective-permute-start | bytes 1179656 | tf_op jit(solution)/shard_map/ppermute | solution.py:23
  358.4 1.9 collective-permute-start.7
  360.8 18.2 %psum.29 = f32[1,32]{1,0:T(1,128)S(1)} all-reduce(f32[1,32]{1,0:T(1,128)S(1)} %bitcast.317), channel_id=1, replica_groups=mesh['tm'=32,'rows'=8] {'rows'}, use_global_device_ids=true, to_apply=%region_5.6 | all-reduce | flops 32 | bytes 256 | tf_op jit(solution)/shard_map/psum | solution.py:55
  379.1 1.2 pad_maximum_fusion.6
  380.4 0.4 select_maximum_fusion
  380.8 2.1 fusion.37
  383.0 2.6 fusion.36
  385.7 5.8 %fusion.35 = (bf16[1,32,16,512]{3,2,0,1:T(8,128)(2,1)S(1)}, bf16[1,32,16,512]{3,2,0,1:T(8,128)(2,1)S(1)}, bf16[1,32,16,512]{3,2,0,1:T(8,128)(2,1)S(1)}, bf16[1,3...) fusion(bf16[27,32,16,512]{3,2,0,1:T(8,128)(2,1)} %bitcast.5), kind=kLoop, calls=%fused_computation.69 | loop fusion | bytes 19922944 | tf_op jit(solution)/shard_map/slice | solution.py:79
  391.7 0.3 fusion.75
  392.1 0.3 fusion.67
  392.5 0.3 fusion.74
  393.2 0.3 fusion.72
  393.6 0.3 fusion.71
  393.9 0.3 fusion.70
  394.3 0.3 fusion.69
  394.7 0.3 fusion.92
  395.0 0.3 fusion.68
  395.4 0.3 fusion.91
  395.7 0.3 fusion.90
  396.1 0.3 fusion.88
  396.8 0.3 fusion.86
  397.2 0.3 fusion.85
  397.6 0.3 fusion.84
  397.9 0.3 fusion.83
  398.6 0.3 fusion.81
  399.0 0.3 fusion.80
  399.4 0.3 fusion.79
  399.7 0.3 fusion.78
  400.4 0.3 fusion.76
  401.1 1.0 fusion.8
  402.1 1.1 fusion.33
  403.3 1.9 collective-permute-start.1
  405.2 4.5 collective-permute-start
  410.1 23.0 %all-reduce.2 = (f32[1,32]{1,0:T(1,128)S(1)}, f32[1,32]{1,0:T(1,128)S(1)}) all-reduce(f32[1,32]{1,0:T(1,128)S(1)} %bitcast.315, f32[1,32]{1,0:T(1,128)S(1)} %bitcast.314), channel_id=1, replica_groups=mesh['tm'=32,'rows'=8] {'rows'}, use_global_device_ids=true, to_apply=%region_11.12 | all-reduce | flops 64 | bytes 512 | tf_op jit(solution)/shard_map/psum | solution.py:104
  433.4 1.4 fusion.63
  435.1 4.1 collective-permute-start.2
  439.2 2.1 collective-permute-start.3
  441.9 11.6 %collective-permute-done.3 = bf16[3,1,128,512]{3,2,1,0:T(8,128)(2,1)S(1)} collective-permute-done((bf16[3,1,128,512]{3,2,1,0:T(8,128)(2,1)S(1)}, bf16[3,1,128,512]{3,2,1,0:T(8,128)(2,1)S(1)}, u32[]{:S(2)}, u32[]{:S(2)}) %collective-permute-start.3) | collective-permute-done | bytes 393248 | tf_op jit(solution)/shard_map/ppermute | solution.py:24
  455.6 0.7 select_maximum_fusion.2
  456.4 0.8 fusion.38
  462.8 1.1 fusion.11
  464.0 1.1 fusion.30
  (218 shorter events, 11.7 us)
Async XLA Ops:
  8.5 11.8 %copy-start.45 = (bf16[1,2,128,512]{3,2,1,0:T(8,128)(2,1)S(1)}, bf16[1,2,128,512]{3,2,1,0:T(8,128)(2,1)}, u32[]{:S(2)}) copy-start(bf16[1,2,128,512]{3,2,1,0:T(8,128)(2,1)} %param.7) | copy-start | bytes 786436
  8.5 21.3 %copy-start.43 = (bf16[1,2,128,512]{3,2,1,0:T(8,128)(2,1)S(1)}, bf16[1,2,128,512]{3,2,1,0:T(8,128)(2,1)}, u32[]{:S(2)}) copy-start(bf16[1,2,128,512]{3,2,1,0:T(8,128)(2,1)} %param.4) | copy-start | bytes 786436
  8.5 374.5 %all-to-all-start = ((bf16[32,27,16,512]{3,2,1,0:T(8,128)(2,1)}), bf16[32,27,16,512]{3,2,1,0:T(8,128)(2,1)}, u32[]{:S(2)}, u32[]{:S(2)}) async-start(bf16[32,27,16,512]{3,2,1,0:T(8,128)(2,1)} %stack.2), calls=%async_computation | async-start | bytes 28311552 | tf_op jit(solution)/shard_map/all_to_all | solution.py:44
  20.3 331.4 %collective-permute-start.4 = (bf16[1,2,128,512]{3,2,1,0:T(8,128)(2,1)S(1)}, bf16[1,2,128,512]{3,2,1,0:T(8,128)(2,1)S(1)}, u32[]{:S(2)}, u32[]{:S(2)}) collective-permute-start(bf16[1,2,128,512]{3,2,1,0:T(8,128)(2,1)S(1)} %copy-done.45), channel_id=1, source_target_pairs={{8,0},{16,8},{24,16},{32,24},{40,32},{48,40},{56,48},{64,56},{72,6... | collective-permute-start | bytes 786440 | tf_op jit(solution)/shard_map/ppermute | solution.py:13
  25.5 326.2 %collective-permute-start.5 = (bf16[1,2,128,512]{3,2,1,0:T(8,128)(2,1)S(1)}, bf16[1,2,128,512]{3,2,1,0:T(8,128)(2,1)S(1)}, u32[]{:S(2)}, u32[]{:S(2)}) collective-permute-start(bf16[1,2,128,512]{3,2,1,0:T(8,128)(2,1)S(1)} %copy-done.45), channel_id=1, source_target_pairs={{16,0},{24,8},{32,16},{40,24},{48,32},{56,40},{64,48},{72,56},{80,... | collective-permute-start | bytes 786440 | tf_op jit(solution)/shard_map/ppermute | solution.py:13
  352.4 26.7 %collective-permute-start.6 = (bf16[3,1,128,512]{3,2,1,0:T(8,128)(2,1)S(1)}, bf16[3,1,128,512]{3,2,1,0:T(8,128)(2,1)S(1)}, u32[]{:S(2)}, u32[]{:S(2)}) collective-permute-start(bf16[3,1,128,512]{3,2,1,0:T(8,128)(2,1)S(1)} %get-tuple-element.85), channel_id=1, source_target_pairs={{0,1},{1,2},{2,3},{3,4},{4,5},{5,6},{6,7},{8,9},{9,10},{10,11},{11... | collective-permute-start | bytes 1179656 | tf_op jit(solution)/shard_map/ppermute | solution.py:23
  358.4 20.7 %collective-permute-start.7 = (bf16[3,1,128,512]{3,2,1,0:T(8,128)(2,1)S(1)}, bf16[3,1,128,512]{3,2,1,0:T(8,128)(2,1)S(1)}, u32[]{:S(2)}, u32[]{:S(2)}) collective-permute-start(bf16[3,1,128,512]{3,2,1,0:T(8,128)(2,1)S(1)} %get-tuple-element.86), channel_id=1, source_target_pairs={{1,0},{2,1},{3,2},{4,3},{5,4},{6,5},{7,6},{9,8},{10,9},{11,10},{12... | collective-permute-start | bytes 1179656 | tf_op jit(solution)/shard_map/ppermute | solution.py:24
  385.6 6.1 %copy-start.4 = (bf16[1,32,16,512]{3,2,0,1:T(8,128)(2,1)}, bf16[1,32,16,512]{3,2,0,1:T(8,128)(2,1)S(1)}, u32[]{:S(2)}) copy-start(bf16[1,32,16,512]{3,2,0,1:T(8,128)(2,1)S(1)} %get-tuple-element.27) | copy-start | bytes 1572868
  385.6 6.8 %copy-start.32 = (bf16[1,32,16,512]{3,2,0,1:T(8,128)(2,1)}, bf16[1,32,16,512]{3,2,0,1:T(8,128)(2,1)S(1)}, u32[]{:S(2)}) copy-start(bf16[1,32,16,512]{3,2,0,1:T(8,128)(2,1)S(1)} %get-tuple-element.28) | copy-start | bytes 1572868
  385.6 7.2 %copy-start.8 = (bf16[1,32,16,512]{3,2,0,1:T(8,128)(2,1)}, bf16[1,32,16,512]{3,2,0,1:T(8,128)(2,1)S(1)}, u32[]{:S(2)}) copy-start(bf16[1,32,16,512]{3,2,0,1:T(8,128)(2,1)S(1)} %get-tuple-element.29) | copy-start | bytes 1572868
  385.7 7.5 %copy-start.12 = (bf16[1,32,16,512]{3,2,0,1:T(8,128)(2,1)}, bf16[1,32,16,512]{3,2,0,1:T(8,128)(2,1)S(1)}, u32[]{:S(2)}) copy-start(bf16[1,32,16,512]{3,2,0,1:T(8,128)(2,1)S(1)} %get-tuple-element.30) | copy-start | bytes 1572868
  385.7 7.9 %copy-start.36 = (bf16[1,32,16,512]{3,2,0,1:T(8,128)(2,1)}, bf16[1,32,16,512]{3,2,0,1:T(8,128)(2,1)S(1)}, u32[]{:S(2)}) copy-start(bf16[1,32,16,512]{3,2,0,1:T(8,128)(2,1)S(1)} %get-tuple-element.31) | copy-start | bytes 1572868
  385.7 8.2 %copy-start.16 = (bf16[1,32,16,512]{3,2,0,1:T(8,128)(2,1)}, bf16[1,32,16,512]{3,2,0,1:T(8,128)(2,1)S(1)}, u32[]{:S(2)}) copy-start(bf16[1,32,16,512]{3,2,0,1:T(8,128)(2,1)S(1)} %get-tuple-element.32) | copy-start | bytes 1572868
  385.7 8.6 %copy-start.20 = (bf16[1,32,16,512]{3,2,0,1:T(8,128)(2,1)}, bf16[1,32,16,512]{3,2,0,1:T(8,128)(2,1)S(1)}, u32[]{:S(2)}) copy-start(bf16[1,32,16,512]{3,2,0,1:T(8,128)(2,1)S(1)} %get-tuple-element.33) | copy-start | bytes 1572868
  385.7 6.0 %copy-start.70 = (bf16[1,2,128,512]{3,2,1,0:T(8,128)(2,1)S(1)}, bf16[1,2,128,512]{3,2,1,0:T(8,128)(2,1)}, u32[]{:S(2)}) copy-start(bf16[1,2,128,512]{3,2,1,0:T(8,128)(2,1)} %get-tuple-element.46) | copy-start | bytes 786436
  385.7 6.4 %copy-start.69 = (bf16[1,2,128,512]{3,2,1,0:T(8,128)(2,1)S(1)}, bf16[1,2,128,512]{3,2,1,0:T(8,128)(2,1)}, u32[]{:S(2)}) copy-start(bf16[1,2,128,512]{3,2,1,0:T(8,128)(2,1)} %get-tuple-element.34) | copy-start | bytes 786436
  385.7 6.7 %copy-start.63 = (bf16[1,2,128,512]{3,2,1,0:T(8,128)(2,1)S(1)}, bf16[1,2,128,512]{3,2,1,0:T(8,128)(2,1)}, u32[]{:S(2)}) copy-start(bf16[1,2,128,512]{3,2,1,0:T(8,128)(2,1)} %get-tuple-element.84) | copy-start | bytes 786436
  391.5 3.1 copy-start.24
  391.5 3.5 copy-start.28
  391.6 3.8 copy-start.38
  391.6 5.2 %copy-start.30 = (bf16[1,32,16,512]{3,2,0,1:T(8,128)(2,1)}, bf16[1,32,16,512]{3,2,0,1:T(8,128)(2,1)S(1)}, u32[]{:S(2)}) copy-start(bf16[1,32,16,512]{3,2,0,1:T(8,128)(2,1)S(1)} %get-tuple-element.15) | copy-start | bytes 1572868
  391.6 5.6 %copy-start = (bf16[1,32,16,512]{3,2,0,1:T(8,128)(2,1)}, bf16[1,32,16,512]{3,2,0,1:T(8,128)(2,1)S(1)}, u32[]{:S(2)}) copy-start(bf16[1,32,16,512]{3,2,0,1:T(8,128)(2,1)S(1)} %get-tuple-element.16) | copy-start | bytes 1572868
  391.6 5.9 %copy-start.2 = (bf16[1,32,16,512]{3,2,0,1:T(8,128)(2,1)}, bf16[1,32,16,512]{3,2,0,1:T(8,128)(2,1)S(1)}, u32[]{:S(2)}) copy-start(bf16[1,32,16,512]{3,2,0,1:T(8,128)(2,1)S(1)} %get-tuple-element.17) | copy-start | bytes 1572868
  391.6 6.3 %copy-start.34 = (bf16[1,32,16,512]{3,2,0,1:T(8,128)(2,1)}, bf16[1,32,16,512]{3,2,0,1:T(8,128)(2,1)S(1)}, u32[]{:S(2)}) copy-start(bf16[1,32,16,512]{3,2,0,1:T(8,128)(2,1)S(1)} %get-tuple-element.18) | copy-start | bytes 1572868
  391.6 6.7 %copy-start.6 = (bf16[1,32,16,512]{3,2,0,1:T(8,128)(2,1)}, bf16[1,32,16,512]{3,2,0,1:T(8,128)(2,1)S(1)}, u32[]{:S(2)}) copy-start(bf16[1,32,16,512]{3,2,0,1:T(8,128)(2,1)S(1)} %get-tuple-element.19) | copy-start | bytes 1572868
  391.6 7.0 %copy-start.10 = (bf16[1,32,16,512]{3,2,0,1:T(8,128)(2,1)}, bf16[1,32,16,512]{3,2,0,1:T(8,128)(2,1)S(1)}, u32[]{:S(2)}) copy-start(bf16[1,32,16,512]{3,2,0,1:T(8,128)(2,1)S(1)} %get-tuple-element.20) | copy-start | bytes 1572868
  391.6 7.4 %copy-start.40 = (bf16[1,32,16,512]{3,2,0,1:T(8,128)(2,1)}, bf16[1,32,16,512]{3,2,0,1:T(8,128)(2,1)S(1)}, u32[]{:S(2)}) copy-start(bf16[1,32,16,512]{3,2,0,1:T(8,128)(2,1)S(1)} %get-tuple-element.21) | copy-start | bytes 1572868
  391.6 7.7 %copy-start.14 = (bf16[1,32,16,512]{3,2,0,1:T(8,128)(2,1)}, bf16[1,32,16,512]{3,2,0,1:T(8,128)(2,1)S(1)}, u32[]{:S(2)}) copy-start(bf16[1,32,16,512]{3,2,0,1:T(8,128)(2,1)S(1)} %get-tuple-element.22) | copy-start | bytes 1572868
  391.6 8.0 %copy-start.18 = (bf16[1,32,16,512]{3,2,0,1:T(8,128)(2,1)}, bf16[1,32,16,512]{3,2,0,1:T(8,128)(2,1)S(1)}, u32[]{:S(2)}) copy-start(bf16[1,32,16,512]{3,2,0,1:T(8,128)(2,1)S(1)} %get-tuple-element.23) | copy-start | bytes 1572868
  391.7 8.4 %copy-start.26 = (bf16[1,32,16,512]{3,2,0,1:T(8,128)(2,1)}, bf16[1,32,16,512]{3,2,0,1:T(8,128)(2,1)S(1)}, u32[]{:S(2)}) copy-start(bf16[1,32,16,512]{3,2,0,1:T(8,128)(2,1)S(1)} %get-tuple-element.24) | copy-start | bytes 1572868
  391.7 8.7 %copy-start.22 = (bf16[1,32,16,512]{3,2,0,1:T(8,128)(2,1)}, bf16[1,32,16,512]{3,2,0,1:T(8,128)(2,1)S(1)}, u32[]{:S(2)}) copy-start(bf16[1,32,16,512]{3,2,0,1:T(8,128)(2,1)S(1)} %get-tuple-element.25) | copy-start | bytes 1572868
  391.7 9.1 %copy-start.42 = (bf16[1,32,16,512]{3,2,0,1:T(8,128)(2,1)}, bf16[1,32,16,512]{3,2,0,1:T(8,128)(2,1)S(1)}, u32[]{:S(2)}) copy-start(bf16[1,32,16,512]{3,2,0,1:T(8,128)(2,1)S(1)} %get-tuple-element.12) | copy-start | bytes 1572868
  391.7 1.8 copy-start.74
  392.1 1.8 copy-start.66
  392.4 1.9 copy-start.65
  392.8 1.9 copy-start.64
  393.2 1.9 copy-start.54
  393.5 1.9 copy-start.52
  396.8 1.9 copy-start.56
  403.3 31.6 %collective-permute-start.1 = (bf16[1,2,128,512]{3,2,1,0:T(8,128)(2,1)S(1)}, bf16[1,2,128,512]{3,2,1,0:T(8,128)(2,1)S(1)}, u32[]{:S(2)}, u32[]{:S(2)}) collective-permute-start(bf16[1,2,128,512]{3,2,1,0:T(8,128)(2,1)S(1)} %get-tuple-element.89), channel_id=1, source_target_pairs={{0,8},{8,16},{16,24},{24,32},{32,40},{40,48},{48,56},{56,64},{64,7... | collective-permute-start | bytes 786440 | tf_op jit(solution)/shard_map/ppermute | solution.py:13
  405.2 29.7 %collective-permute-start = (bf16[1,2,128,512]{3,2,1,0:T(8,128)(2,1)S(1)}, bf16[1,2,128,512]{3,2,1,0:T(8,128)(2,1)S(1)}, u32[]{:S(2)}, u32[]{:S(2)}) collective-permute-start(bf16[1,2,128,512]{3,2,1,0:T(8,128)(2,1)S(1)} %get-tuple-element.89), channel_id=1, source_target_pairs={{0,16},{8,24},{16,32},{24,40},{32,48},{40,56},{48,64},{56,72},{64,... | collective-permute-start | bytes 786440 | tf_op jit(solution)/shard_map/ppermute | solution.py:13
  433.4 7.9 %copy-start.41 = (bf16[1,32,16,512]{3,2,0,1:T(8,128)(2,1)S(1)}, bf16[1,32,16,512]{3,2,0,1:T(8,128)(2,1)}, u32[]{:S(2)}) copy-start(bf16[1,32,16,512]{3,2,0,1:T(8,128)(2,1)} %copy-done.40) | copy-start | bytes 1572868
  433.4 8.2 %copy-start.37 = (bf16[1,32,16,512]{3,2,0,1:T(8,128)(2,1)S(1)}, bf16[1,32,16,512]{3,2,0,1:T(8,128)(2,1)}, u32[]{:S(2)}) copy-start(bf16[1,32,16,512]{3,2,0,1:T(8,128)(2,1)} %copy-done.36) | copy-start | bytes 1572868
  435.0 18.6 %copy-start.39 = (bf16[1,32,16,512]{3,2,0,1:T(8,128)(2,1)S(1)}, bf16[1,32,16,512]{3,2,0,1:T(8,128)(2,1)}, u32[]{:S(2)}) copy-start(bf16[1,32,16,512]{3,2,0,1:T(8,128)(2,1)} %copy-done.38) | copy-start | bytes 1572868
  435.1 18.9 %copy-start.33 = (bf16[1,32,16,512]{3,2,0,1:T(8,128)(2,1)S(1)}, bf16[1,32,16,512]{3,2,0,1:T(8,128)(2,1)}, u32[]{:S(2)}) copy-start(bf16[1,32,16,512]{3,2,0,1:T(8,128)(2,1)} %copy-done.32) | copy-start | bytes 1572868
  435.1 19.5 %collective-permute-start.2 = (bf16[3,1,128,512]{3,2,1,0:T(8,128)(2,1)S(1)}, bf16[3,1,128,512]{3,2,1,0:T(8,128)(2,1)S(1)}, u32[]{:S(2)}, u32[]{:S(2)}) collective-permute-start(bf16[3,1,128,512]{3,2,1,0:T(8,128)(2,1)S(1)} %get-tuple-element.87), channel_id=1, source_target_pairs={{0,1},{1,2},{2,3},{3,4},{4,5},{5,6},{6,7},{8,9},{9,10},{10,11},{11... | collective-permute-start | bytes 1179656 | tf_op jit(solution)/shard_map/ppermute | solution.py:23
  439.2 14.4 %collective-permute-start.3 = (bf16[3,1,128,512]{3,2,1,0:T(8,128)(2,1)S(1)}, bf16[3,1,128,512]{3,2,1,0:T(8,128)(2,1)S(1)}, u32[]{:S(2)}, u32[]{:S(2)}) collective-permute-start(bf16[3,1,128,512]{3,2,1,0:T(8,128)(2,1)S(1)} %get-tuple-element.88), channel_id=1, source_target_pairs={{1,0},{2,1},{3,2},{4,3},{5,4},{6,5},{7,6},{9,8},{10,9},{11,10},{12... | collective-permute-start | bytes 1179656 | tf_op jit(solution)/shard_map/ppermute | solution.py:24
  441.3 13.0 %copy-start.35 = (bf16[1,32,16,512]{3,2,0,1:T(8,128)(2,1)S(1)}, bf16[1,32,16,512]{3,2,0,1:T(8,128)(2,1)}, u32[]{:S(2)}) copy-start(bf16[1,32,16,512]{3,2,0,1:T(8,128)(2,1)} %copy-done.34) | copy-start | bytes 1572868
  (37 other events, 55.8 us)
